TPU v7x, 128 devices: a whole 4x4x4 slice. The times are simulated.
128 devices in a mesh: shard: 8 (over y, core), tensor: 4 (over z), section: 4 (over x).
Axes of the slice: x: 4, y: 4, z: 4, core: 2. Of those that a mesh axis runs over, the one named last changes fastest.
Arguments:
- activations: bfloat16 [4, 16384, 2048], P('section', 'shard'), may hold values from -500 to 500, as said below
- out_grad: bfloat16 [4, 16384, 8192], P('section', 'shard', 'tensor'), may hold values from -30 to 30, as said below
- basis: float32 [4, 2048, 256], P('section', 'shard'), may hold values from -0.125 to 0.125
- first_moment: float32 [4, 256, 8192], P('section', 'shard', 'tensor'), may hold values from -6 to 6
- second_moment: float32 [4, 256, 8192], P('section', 'shard', 'tensor'), may hold values from 0.5 to 2
- gain_partial: float32 [4, 8, 2048], P('section', 'shard'), may hold values from -4096 to 4096
- gain_first: float32 [4, 2048], P('section', 'shard'), may hold values from -6 to 6
- gain_second: float32 [4, 2048], P('section', 'shard'), may hold values from 0.5 to 2
Outputs:
- update: float32 [4, 2048, 8192], P('section', 'shard', 'tensor')
- first_out: float32 [4, 256, 8192], P('section', 'shard', 'tensor')
- second_out: float32 [4, 256, 8192], P('section', 'shard', 'tensor')
- new_basis: float32 [4, 2048, 256], P('section', ('shard', 'tensor'))
- gain_step: float32 [4, 2048], P('section', 'shard')
- gain_first_out: float32 [4, 2048], P('section', 'shard')
- gain_second_out: float32 [4, 2048], P('section', 'shard')
Inputs may be any that keep to these rules, and one draw needn't show every extreme that they name: Real-valued activations whose column scales differ from column to column. `out_grad`: Real-valued gradients whose column scales differ from column to column.
All inputs are finite; a program needn't handle non-finite values.
Results may differ from a plain program's by a relative error of at most 0.0003.
Values sent between devices are 32-bit elements; how exact they have to be, the bound alone decides.
No kernel may reach another device: no remote copies, remote signals or barrier semaphores. Data moves between devices by JAX's collectives and lax.ppermute only.
A program may use at most 128 MiB of HBM per device.

v0:
```python
import jax
import jax.numpy as jnp
from jax import lax
from jax.sharding import PartitionSpec as P

D = 2048
FF = 8192
NS_STEPS = 5
STEP = 8
exact_mode = lax.Precision.HIGHEST
beta_one = 0.9
beta_two = 0.999
adam_eps = 1e-08
clip_eps = 1e-06
ns_eps = 1e-07
coef_first = 3.4445
coef_second = -4.775
coef_third = 2.0315


def adam_direction(clipped, first_old, second_old):
    first_new = beta_one * first_old + (1.0 - beta_one) * clipped
    second_new = beta_two * second_old + (1.0 - beta_two) * clipped * clipped
    direction = (
        first_new
        / (1.0 - beta_one**STEP)
        / (jnp.sqrt(second_new / (1.0 - beta_two**STEP)) + adam_eps)
    )
    return (first_new, second_new, direction)


def ns_update(current, gram):
    mixer = coef_second * gram + coef_third * jnp.dot(gram, gram, precision=exact_mode)
    return coef_first * current + jnp.dot(current, mixer, precision=exact_mode)


def gram_of(block):
    local_gram = jnp.dot(block.T, block, precision=exact_mode)
    return lax.psum(local_gram, ("shard", "tensor"))


def shards(
    activations, out_grad, basis, first_moment, second_moment, gain_partial, gain_first, gain_second
):
    tensors = lax.axis_size("tensor")
    shard_pos = lax.axis_index("shard")
    layer_count = activations.shape[0]
    rows_here = basis.shape[1]
    rank_rows = first_moment.shape[1]
    cols_here = out_grad.shape[2]
    layer_index = 0
    tokens_in = activations[layer_index]
    grads_out = out_grad[layer_index]
    basis_here = basis[layer_index]

    def row_term(start, count, tokens_in=tokens_in, grads_out=grads_out):
        return lax.dot_general(
            tokens_in, grads_out, (((0,), (0,)), ((), ())), preferred_element_type=jnp.float32
        )

    grad_block = lax.psum_scatter(
        row_term(jnp.int32(0), lax.axis_size("shard") * rows_here),
        "shard",
        scatter_dimension=0,
        tiled=True,
    )
    part_proj = jnp.dot(basis_here.T, grad_block, precision=exact_mode)
    proj_full, gain_total = lax.psum((part_proj, gain_partial[layer_index, 0]), "shard")
    proj_rows = lax.dynamic_slice_in_dim(proj_full, shard_pos * rank_rows, rank_rows, 0)
    square_sum = jnp.sum(grad_block * grad_block)

    def refresh_term(start, count, grad_block=grad_block, proj_full=proj_full):
        return lax.dot_general(
            grad_block, proj_full, (((1,), (1,)), ((), ())), precision=exact_mode
        )

    refreshed = lax.psum_scatter(
        refresh_term(jnp.int32(0), lax.axis_size("tensor") * (rows_here // tensors)),
        "tensor",
        scatter_dimension=0,
        tiled=True,
    )
    kept_list = [basis_here]
    gain_own = lax.dynamic_slice_in_dim(gain_total, shard_pos * rows_here, rows_here, 0)
    square_sum = square_sum + jnp.sum(gain_own * gain_own) / float(tensors)
    proj_list = [proj_rows]
    gain_list = [gain_own]
    refresh_list = [refreshed]
    total_sq = lax.psum(square_sum, ("shard", "tensor", "section"))
    entry_count = float(lax.axis_size("section") * layer_count * (D * FF + D))
    clip = jnp.minimum(1.0, lax.rsqrt(total_sq / entry_count + clip_eps))
    layer_index = 0
    first_new, second_new, direction = adam_direction(
        clip * proj_list[layer_index], first_moment[layer_index], second_moment[layer_index]
    )
    firsts = [first_new]
    seconds = [second_new]
    kept_basis = kept_list[layer_index]

    def fold_rows(total, piece, start, kept_basis=kept_basis):
        return jnp.dot(kept_basis, piece, precision=exact_mode)

    empty = jnp.zeros((rows_here, cols_here), jnp.float32)
    update_here = fold_rows(
        empty, lax.all_gather(direction, "shard", axis=0, tiled=True), jnp.int32(0)
    )
    updates = [update_here]
    refreshed = refresh_list[layer_index]
    frob = lax.psum(jnp.sum(refreshed * refreshed), ("shard", "tensor"))
    current = refreshed / jnp.sqrt(frob + ns_eps)
    gram = gram_of(current)
    for step_index in range(NS_STEPS):
        current = ns_update(current, gram)
        if step_index + 1 < NS_STEPS:
            gram = gram_of(current)
    bases = [current]
    gain_first_new, gain_second_new, gain_dir = adam_direction(
        clip * gain_list[layer_index], gain_first[layer_index], gain_second[layer_index]
    )
    gain_steps = [gain_dir]
    gain_firsts = [gain_first_new]
    gain_seconds = [gain_second_new]
    return (
        jnp.stack(updates),
        jnp.stack(firsts),
        jnp.stack(seconds),
        jnp.stack(bases),
        jnp.stack(gain_steps),
        jnp.stack(gain_firsts),
        jnp.stack(gain_seconds),
    )


def solution(mesh):
    placed = (
        P("section", "shard", None),
        P("section", "shard", "tensor"),
        P("section", "shard", None),
        P("section", "shard", "tensor"),
        P("section", "shard", "tensor"),
        P("section", "shard", None),
        P("section", "shard"),
        P("section", "shard"),
    )
    return jax.shard_map(
        shards,
        mesh=mesh,
        in_specs=placed,
        out_specs=(
            P("section", "shard", "tensor"),
            P("section", "shard", "tensor"),
            P("section", "shard", "tensor"),
            P("section", ("shard", "tensor"), None),
            P("section", "shard"),
            P("section", "shard"),
            P("section", "shard"),
        ),
        check_vma=False,
    )
```

profile of v0, /device:TPU:1, one launch (start us, length us, event | category | flops | bytes accessed | tf_op | source)
XLA Modules:
  0.0 854.7 jit_solution(13370359571268590590)
XLA Ops:
  7.2 24.3 %fusion = f32[2048,2048]{1,0:T(8,128)} fusion(bf16[1,2048,2048]{2,1,0:T(8,128)(2,1)} %param.9, bf16[1,2048,2048]{2,1,0:T(8,128)(2,1)} %param.8), kind=kOutput, calls=%fused_computation | convolution fusion | flops 17179869184 | bytes 33554432 | tf_op jit(solution)/shard_map/dot_general | solution.py:57
  31.6 94.5 %reduce-scatter.3.cloned.1.call-done = f32[256,2048]{1,0:T(8,128)} async-done(((f32[2048,2048]{1,0:T(8,128)}), f32[256,2048]{1,0:T(8,128)}) %reduce-scatter.3.cloned.1.call-update) | async-done | bytes 2097168 | tf_op jit(solution)/shard_map/reduce_scatter | solution.py:61
  126.1 6.4 convolution_bitcast_fusion.1
  132.6 64.0 %all-reduce.7.cloned.1.call-done = f32[256,2048]{0,1:T(8,128)} async-done(((f32[256,2048]{0,1:T(8,128)}), f32[256,2048]{0,1:T(8,128)}) %all-reduce.7.cloned.1.call-update) | async-done | bytes 2097168 | tf_op jit(solution)/shard_map/psum | solution.py:68
  196.6 4.2 fusion.17
  200.9 20.4 %reduce-scatter.5.cloned.1.call-done = f32[64,256]{1,0:T(8,128)} async-done(((f32[256,256]{1,0:T(8,128)}), f32[64,256]{1,0:T(8,128)}) %reduce-scatter.5.cloned.1.call-update) | async-done | bytes 65552 | tf_op jit(solution)/shard_map/reduce_scatter | solution.py:77
  222.7 62.0 %psum.66 = f32[]{:T(128)} all-reduce(f32[]{:T(128)} %multiply_reduce_fusion.1), channel_id=1, replica_groups=mesh['shard'=8,'tensor'=4,'section'=4] {'shard','tensor'}, use_global_device_ids=true, to_apply=%region_8.0 | all-reduce | flops 1 | bytes 8 | tf_op jit(solution)/shard_map/psum | solution.py:109
  285.4 2.0 fusion.14
  287.5 104.3 %all-reduce.9.cloned.1.call-done = f32[256,256]{1,0:T(8,128)} async-done(((f32[256,256]{1,0:T(8,128)}), f32[256,256]{1,0:T(8,128)}) %all-reduce.9.cloned.1.call-update) | async-done | bytes 262160 | tf_op jit(solution)/shard_map/psum | solution.py:39
  395.8 101.9 %all-reduce.11.cloned.1.call-done = f32[256,256]{1,0:T(8,128)} async-done(((f32[256,256]{1,0:T(8,128)}), f32[256,256]{1,0:T(8,128)}) %all-reduce.11.cloned.1.call-update) | async-done | bytes 262160 | tf_op jit(solution)/shard_map/psum | solution.py:39
  501.9 2.3 copy.21
  504.2 13.5 %psum.63 = f32[2048]{0:T(1024)S(1)} all-reduce(f32[2048]{0:T(1024)S(1)} %bitcast.72), channel_id=1, replica_groups=mesh['shard'=8,'tensor'=4,'section'=4] {'shard'}, use_global_device_ids=true, to_apply=%region_2.0 | all-reduce | flops 2048 | bytes 16384 | tf_op jit(solution)/shard_map/psum | solution.py:68
  519.0 84.3 %all-reduce.13.cloned.1.call-done = f32[256,256]{1,0:T(8,128)} async-done(((f32[256,256]{1,0:T(8,128)}), f32[256,256]{1,0:T(8,128)}) %all-reduce.13.cloned.1.call-update) | async-done | bytes 262160 | tf_op jit(solution)/shard_map/psum | solution.py:39
  603.3 1.5 fusion.5
  608.2 65.9 %psum.64 = f32[]{:T(128)} all-reduce(f32[]{:T(128)S(6)} %add.92), channel_id=1, replica_groups=mesh['shard'=8,'tensor'=4,'section'=4] {'shard','tensor','section'}, use_global_device_ids=true, to_apply=%region_4.0 | all-reduce | flops 1 | bytes 8 | tf_op jit(solution)/shard_map/psum | solution.py:89
  674.7 34.5 %all-reduce.15.cloned.1.call-done = f32[256,256]{1,0:T(8,128)} async-done(((f32[256,256]{1,0:T(8,128)}), f32[256,256]{1,0:T(8,128)}) %all-reduce.15.cloned.1.call-update) | async-done | bytes 262160 | tf_op jit(solution)/shard_map/psum | solution.py:39
  709.2 1.5 fusion.4
  712.2 3.3 fusion.13
  715.5 2.3 copy.22
  720.6 93.8 %all-reduce.17.cloned.1.call-done = f32[256,256]{1,0:T(8,128)} async-done(((f32[256,256]{1,0:T(8,128)}), f32[256,256]{1,0:T(8,128)}) %all-reduce.17.cloned.1.call-update) | async-done | bytes 262160 | tf_op jit(solution)/shard_map/psum | solution.py:39
  814.4 1.5 fusion.3
  816.9 24.5 %all-gather.2.cloned.1.call-done = f32[256,2048]{1,0:T(8,128)} async-done(((f32[32,2048]{1,0:T(8,128)}), f32[256,2048]{1,0:T(8,128)}) %all-gather.2.cloned.1.call-update) | async-done | bytes 2097168 | tf_op jit(solution)/shard_map/all_gather | solution.py:105
  841.4 5.0 convolution_bitcast_fusion
  846.4 1.8 copy.23
  (52 shorter events, 18.2 us)
Async XLA Ops:
  7.2 119.0 %copy-start = (f32[1,256,256]{2,1,0:T(8,128)S(1)}, f32[1,256,256]{2,1,0:T(8,128)}, u32[]{:S(2)}) copy-start(f32[1,256,256]{2,1,0:T(8,128)} %param.10) | copy-start | bytes 786436
  7.2 119.0 %reduce-scatter.3.cloned.1.call-start = ((), (), s32[]{:S(2)}) async-start(), calls=%async_computation.2 | async-start | bytes 18874368 | tf_op jit(solution)/shard_map/reduce_scatter | solution.py:61
  31.5 165.1 %all-reduce.7.cloned.1.call-start = ((), (), s32[]{:S(2)}) async-start(), calls=%async_computation.3 | async-start | bytes 4194304 | tf_op jit(solution)/shard_map/psum | solution.py:68
  132.5 64.1 %copy-start.1 = (f32[256,2048]{1,0:T(8,128)S(1)}, f32[256,2048]{1,0:T(8,128)}, u32[]{:S(2)}) copy-start(f32[256,2048]{1,0:T(8,128)} %reduce-scatter.3.cloned.1.call-done) | copy-start | bytes 6291460
  132.5 88.7 %reduce-scatter.5.cloned.1.call-start = ((), (), s32[]{:S(2)}) async-start(), calls=%async_computation.5 | async-start | bytes 327680 | tf_op jit(solution)/shard_map/reduce_scatter | solution.py:77
  200.8 191.0 %all-reduce.9.cloned.1.call-start = ((), (), s32[]{:S(2)}) async-start(), calls=%async_computation.6 | async-start | bytes 524288 | tf_op jit(solution)/shard_map/psum | solution.py:39
  287.4 210.3 %all-reduce.11.cloned.1.call-start = ((), (), s32[]{:S(2)}) async-start(), calls=%async_computation.7 | async-start | bytes 524288 | tf_op jit(solution)/shard_map/psum | solution.py:39
  395.6 108.6 %copy-start.4 = (f32[1,1,2048]{2,1,0:T(1,128)S(1)}, f32[1,1,2048]{2,1,0:T(1,128)}, u32[]{:S(2)}) copy-start(f32[1,1,2048]{2,1,0:T(1,128)} %param.13) | copy-start | bytes 24580
  395.6 207.8 %all-reduce.13.cloned.1.call-start = ((), (), s32[]{:S(2)}) async-start(), calls=%async_computation.8 | async-start | bytes 524288 | tf_op jit(solution)/shard_map/psum | solution.py:39
  500.6 208.6 %all-reduce.15.cloned.1.call-start = ((), (), s32[]{:S(2)}) async-start(), calls=%async_computation.9 | async-start | bytes 524288 | tf_op jit(solution)/shard_map/psum | solution.py:39
  606.2 208.2 %all-reduce.17.cloned.1.call-start = ((), (), s32[]{:S(2)}) async-start(), calls=%async_computation.10 | async-start | bytes 524288 | tf_op jit(solution)/shard_map/psum | solution.py:39
  607.4 104.8 %copy-start.2 = (f32[1,32,2048]{1,2,0:T(8,128)S(1)}, f32[1,32,2048]{1,2,0:T(8,128)}, u32[]{:S(2)}) copy-start(f32[1,32,2048]{1,2,0:T(8,128)} %copy.21) | copy-start | bytes 786436
  712.1 5.7 copy-start.5
  712.1 5.8 copy-start.6
  712.1 129.2 %all-gather.2.cloned.1.call-start = ((), (), s32[]{:S(2)}) async-start(), calls=%async_computation.4 | async-start | bytes 2359296 | tf_op jit(solution)/shard_map/all_gather | solution.py:105
  715.5 3.1 copy-start.3
Sparse Core Ops, SparseCore 0:
  31.7 94.4 reduce-scatter.2
  132.6 63.9 all-reduce.6
  200.9 20.2 reduce-scatter.4
  287.6 104.1 all-reduce.8
  395.7 101.9 all-reduce.10
  501.4 101.9 all-reduce.12
  607.1 102.0 all-reduce.14
  712.4 101.9 all-reduce.16
  816.2 25.1 all-gather.1
where the time goes:
time: 855 us
  waiting for transfers between devices  622 us (73%)
  blocking collectives  141 us (16%)
  matrix products  56.7 us (7%)
  between operations  16.8 us (2%)
  local copies, waits for them, and re-layouts  9.74 us (1%)
    psum x5, waiting for transfers between devices, gram_of(): return lax.psum(local_gram, ('shard', 'tensor'))  419 us
    reduce_scatter x1, waiting for transfers between devices, shards(): lax.psum_scatter(row_term(jnp.int32(0), lax.axis_size('shard') * rows_her...  94.5 us
    psum x1, blocking collectives, shards(): total_sq = lax.psum(square_sum, ('shard', 'tensor', 'section'))  65.9 us
    psum x1, waiting for transfers between devices, shards(): lax.psum((part_proj, gain_partial[layer_index, 0]), 'shard')  64 us
    psum x1, blocking collectives, shards(): frob = lax.psum(jnp.sum(refreshed * refreshed), ('shard', 'tensor'))  62 us
    all_gather x1, waiting for transfers between devices, shards(): lax.all_gather(direction, 'shard', axis=0, tiled=True)  24.5 us
    dot_general x1, matrix products, row_term(): lax.dot_general(tokens_in, grads_out, (((0,), (0,)), ((), ())), preferred...  24.3 us
    reduce_scatter x1, waiting for transfers between devices, shards(): lax.psum_scatter(refresh_term(jnp.int32(0), lax.axis_size('tensor') * (ro...  20.4 us
  transfers between devices with their start and end apart: 9, of which 9 were waited for; matrix products, arithmetic and copies ran while one was open for 2% of the time, Pallas kernels for 0%

commit v1 on v0

--- a/solution.py
+++ b/solution.py
@@ -101,9 +101,35 @@
         return jnp.dot(kept_basis, piece, precision=exact_mode)
 
     empty = jnp.zeros((rows_here, cols_here), jnp.float32)
-    update_here = fold_rows(
-        empty, lax.all_gather(direction, "shard", axis=0, tiled=True), jnp.int32(0)
-    )
+
+    def form_the_pages(slab_in):
+        after, z_new, block_next = (
+            jax.lax.axis_size("shard"),
+            jax.lax.axis_index("shard"),
+            slab_in.shape[0],
+        )
+        pool = tuple((j0 * after if at == 0 else j0 for at, j0 in enumerate(slab_in.shape)))
+        p_next = lax.dynamic_update_slice_in_dim(
+            jnp.zeros(pool, slab_in.dtype), slab_in, z_new * block_next, axis=0
+        )
+        x_new = opened = slab_in
+        for idx in [*range(1, after // 2 + 1)]:
+            x_new = jax.lax.ppermute(
+                x_new, "shard", tuple(((at, (at + 1) % after) for at in range(after)))
+            )
+            p_next = lax.dynamic_update_slice_in_dim(
+                p_next, x_new, (z_new - idx) % after * block_next, axis=0
+            )
+            if 2 * idx < after:
+                opened = jax.lax.ppermute(
+                    opened, "shard", tuple(((at, (at - 1) % after) for at in range(after)))
+                )
+                p_next = lax.dynamic_update_slice_in_dim(
+                    p_next, opened, (z_new + idx) % after * block_next, axis=0
+                )
+        return p_next
+
+    update_here = fold_rows(empty, form_the_pages(direction), jnp.int32(0))
     updates = [update_here]
     refreshed = refresh_list[layer_index]
     frob = lax.psum(jnp.sum(refreshed * refreshed), ("shard", "tensor"))

time: 855 us -> 888 us (1.039)
  local copies, waits for them, and re-layouts: 9.74 us -> 79.7 us
  waiting for transfers between devices: 622 us -> 578 us
    dynamic_update_slice x0 -> x8, local copies, waits for them, and re-layouts: none -> 59.4 us  [the longest x4 26.2 us: form_the_pages(): lax.dynamic_update_slice_in_dim(p_next, x_new, (z_new - idx) % after * bl...]
    all_gather x1 -> x0, waiting for transfers between devices: 24.5 us -> none  [shards(): lax.all_gather(direction, 'shard', axis=0, tiled=True)]
    reduce_scatter x1, waiting for transfers between devices: 20.4 us -> 0.02 us  [shards(): lax.psum_scatter(refresh_term(jnp.int32(0), lax.axis_size('tensor') * (ro...]
    ppermute x0 -> x7, local copies, waits for them, and re-layouts: none -> 8.95 us  [the longest x4 5.11 us: form_the_pages(): jax.lax.ppermute(x_new, 'shard', tuple(((at, (at + 1) % after) for at in...]
  transfers between devices with their start and end apart: 9 -> 15, of which waited for: 9 -> 7; matrix products, arithmetic and copies ran while one was open for 2% -> 11% of each run, Pallas kernels for 0% -> 0%
where the time goes in v1:
time: 888 us; the launch traced here: 887 us
  waiting for transfers between devices  578 us (65%)
  blocking collectives  142 us (16%)
  local copies, waits for them, and re-layouts  79.7 us (9%)
  matrix products  54.1 us (6%)
  between operations  17.3 us (2%)
    psum x5, waiting for transfers between devices, gram_of(): return lax.psum(local_gram, ('shard', 'tensor'))  419 us
    reduce_scatter x1, waiting for transfers between devices, shards(): lax.psum_scatter(row_term(jnp.int32(0), lax.axis_size('shard') * rows_her...  94.5 us
    psum x1, blocking collectives, shards(): total_sq = lax.psum(square_sum, ('shard', 'tensor', 'section'))  66 us
    psum x1, waiting for transfers between devices, shards(): lax.psum((part_proj, gain_partial[layer_index, 0]), 'shard')  64 us
    psum x1, blocking collectives, shards(): frob = lax.psum(jnp.sum(refreshed * refreshed), ('shard', 'tensor'))  61.2 us
    dynamic_update_slice x4, local copies, waits for them, and re-layouts, form_the_pages(): lax.dynamic_update_slice_in_dim(p_next, x_new, (z_new - idx) % after * bl...  26.2 us
    dot_general x1, matrix products, row_term(): lax.dot_general(tokens_in, grads_out, (((0,), (0,)), ((), ())), preferred...  24.3 us
    dynamic_update_slice x3, local copies, waits for them, and re-layouts, form_the_pages(): lax.dynamic_update_slice_in_dim(p_next, opened, (z_new + idx) % after * b...  23.6 us
  transfers between devices with their start and end apart: 15, of which 7 were waited for; matrix products, arithmetic and copies ran while one was open for 11% of the time, Pallas kernels for 0%

profile of v1, /device:TPU:1, one launch (start us, length us, event | category | flops | bytes accessed | tf_op | source)
XLA Modules:
  0.0 887.1 jit_solution(4836384813311363831)
XLA Ops:
  7.2 24.3 %fusion = f32[2048,2048]{1,0:T(8,128)} fusion(bf16[1,2048,2048]{2,1,0:T(8,128)(2,1)} %param.9, bf16[1,2048,2048]{2,1,0:T(8,128)(2,1)} %param.8), kind=kOutput, calls=%fused_computation | convolution fusion | flops 17179869184 | bytes 33554432 | tf_op jit(solution)/shard_map/dot_general | solution.py:57
  31.6 94.5 %reduce-scatter.3.cloned.1.call-done = f32[256,2048]{1,0:T(8,128)} async-done(((f32[2048,2048]{1,0:T(8,128)}), f32[256,2048]{1,0:T(8,128)}) %reduce-scatter.3.cloned.1.call-update) | async-done | bytes 2097168 | tf_op jit(solution)/shard_map/reduce_scatter | solution.py:61
  126.1 6.4 convolution_bitcast_fusion.1
  132.6 64.0 %all-reduce.7.cloned.1.call-done = f32[256,2048]{0,1:T(8,128)} async-done(((f32[256,2048]{0,1:T(8,128)}), f32[256,2048]{0,1:T(8,128)}) %all-reduce.7.cloned.1.call-update) | async-done | bytes 2097168 | tf_op jit(solution)/shard_map/psum | solution.py:68
  196.6 4.2 fusion.17
  204.5 14.5 %psum.63 = f32[2048]{0:T(1024)S(1)} all-reduce(f32[2048]{0:T(1024)S(1)} %bitcast.72), channel_id=1, replica_groups=mesh['shard'=8,'tensor'=4,'section'=4] {'shard'}, use_global_device_ids=true, to_apply=%region_2.0 | all-reduce | flops 2048 | bytes 16384 | tf_op jit(solution)/shard_map/psum | solution.py:68
  222.2 66.0 %psum.64 = f32[]{:T(128)} all-reduce(f32[]{:T(128)S(6)} %add.149), channel_id=1, replica_groups=mesh['shard'=8,'tensor'=4,'section'=4] {'shard','tensor','section'}, use_global_device_ids=true, to_apply=%region_4.0 | all-reduce | flops 1 | bytes 8 | tf_op jit(solution)/shard_map/psum | solution.py:89
  290.5 61.2 %psum.66 = f32[]{:T(128)} all-reduce(f32[]{:T(128)} %multiply_reduce_fusion.1), channel_id=1, replica_groups=mesh['shard'=8,'tensor'=4,'section'=4] {'shard','tensor'}, use_global_device_ids=true, to_apply=%region_8.9 | all-reduce | flops 1 | bytes 8 | tf_op jit(solution)/shard_map/psum | solution.py:135
  354.5 3.6 fusion.13
  358.4 5.0 collective-permute-start.1
  363.4 92.7 %all-reduce.9.cloned.1.call-done = f32[256,256]{1,0:T(8,128)} async-done(((f32[256,256]{1,0:T(8,128)}), f32[256,256]{1,0:T(8,128)}) %all-reduce.9.cloned.1.call-update) | async-done | bytes 262160 | tf_op jit(solution)/shard_map/psum | solution.py:39
  460.4 101.4 %all-reduce.11.cloned.1.call-done = f32[256,256]{1,0:T(8,128)} async-done(((f32[256,256]{1,0:T(8,128)}), f32[256,256]{1,0:T(8,128)}) %all-reduce.11.cloned.1.call-update) | async-done | bytes 262160 | tf_op jit(solution)/shard_map/psum | solution.py:39
  565.9 101.5 %all-reduce.13.cloned.1.call-done = f32[256,256]{1,0:T(8,128)} async-done(((f32[256,256]{1,0:T(8,128)}), f32[256,256]{1,0:T(8,128)}) %all-reduce.13.cloned.1.call-update) | async-done | bytes 262160 | tf_op jit(solution)/shard_map/psum | solution.py:39
  671.3 9.5 %dynamic_update_slice.24 = f32[256,2048]{0,1:T(8,128)S(1)} dynamic-update-slice(f32[256,2048]{0,1:T(8,128)S(1)} %broadcast_in_dim.3, f32[32,2048]{0,1:T(8,128)S(1)} %get-tuple-element.25, s32[]{:T(128)S(6)} %select_n.60, s32[]{:T(128)} %constant.85.clone.1) | dynamic-update-slice | bytes 524292 | tf_op jit(solution)/shard_map/dynamic_update_slice | solution.py:112
  686.6 8.0 dynamic_update_slice.25
  695.9 9.5 %dynamic_update_slice.26 = f32[256,2048]{0,1:T(8,128)S(1)} dynamic-update-slice(f32[256,2048]{0,1:T(8,128)S(1)} %dynamic_update_slice.25, f32[32,2048]{0,1:T(8,128)S(1)} %copy.25, s32[]{:T(128)S(6)} %select_n.64, s32[]{:T(128)} %constant.85.clone.1) | dynamic-update-slice | bytes 524292 | tf_op jit(solution)/shard_map/dynamic_update_slice | solution.py:127
  706.7 6.1 dynamic_update_slice.27
  714.1 9.5 %dynamic_update_slice.28 = f32[256,2048]{0,1:T(8,128)S(1)} dynamic-update-slice(f32[256,2048]{0,1:T(8,128)S(1)} %dynamic_update_slice.27, f32[32,2048]{0,1:T(8,128)S(1)} %copy.27, s32[]{:T(128)S(6)} %select_n.68, s32[]{:T(128)} %constant.85.clone.1) | dynamic-update-slice | bytes 524292 | tf_op jit(solution)/shard_map/dynamic_update_slice | solution.py:127
  724.9 6.1 dynamic_update_slice.29
  732.3 4.5 dynamic_update_slice.30
  738.0 34.6 %all-reduce.15.cloned.1.call-done = f32[256,256]{1,0:T(8,128)} async-done(((f32[256,256]{1,0:T(8,128)}), f32[256,256]{1,0:T(8,128)}) %all-reduce.15.cloned.1.call-update) | async-done | bytes 262160 | tf_op jit(solution)/shard_map/psum | solution.py:39
  776.9 6.1 dynamic_update_slice.31
  783.0 3.2 convolution_bitcast_fusion
  789.1 88.8 %all-reduce.17.cloned.1.call-done = f32[256,256]{1,0:T(8,128)} async-done(((f32[256,256]{1,0:T(8,128)}), f32[256,256]{1,0:T(8,128)}) %all-reduce.17.cloned.1.call-update) | async-done | bytes 262160 | tf_op jit(solution)/shard_map/psum | solution.py:39
  (81 shorter events, 44.4 us)
Async XLA Ops:
  7.2 119.0 %copy-start = (f32[1,256,256]{2,1,0:T(8,128)S(1)}, f32[1,256,256]{2,1,0:T(8,128)}, u32[]{:S(2)}) copy-start(f32[1,256,256]{2,1,0:T(8,128)} %param.10) | copy-start | bytes 786436
  7.2 119.0 %reduce-scatter.3.cloned.1.call-start = ((), (), s32[]{:S(2)}) async-start(), calls=%async_computation.2 | async-start | bytes 18874368 | tf_op jit(solution)/shard_map/reduce_scatter | solution.py:61
  31.5 165.1 %all-reduce.7.cloned.1.call-start = ((), (), s32[]{:S(2)}) async-start(), calls=%async_computation.3 | async-start | bytes 4194304 | tf_op jit(solution)/shard_map/psum | solution.py:68
  132.5 64.1 %copy-start.1 = (f32[256,2048]{1,0:T(8,128)S(1)}, f32[256,2048]{1,0:T(8,128)}, u32[]{:S(2)}) copy-start(f32[256,2048]{1,0:T(8,128)} %reduce-scatter.3.cloned.1.call-done) | copy-start | bytes 6291460
  132.5 156.5 %reduce-scatter.5.cloned.1.call-start = ((), (), s32[]{:S(2)}) async-start(), calls=%async_computation.4 | async-start | bytes 327680 | tf_op jit(solution)/shard_map/reduce_scatter | solution.py:77
  200.8 3.8 copy-start.5
  200.8 255.3 %all-reduce.9.cloned.1.call-start = ((), (), s32[]{:S(2)}) async-start(), calls=%async_computation.5 | async-start | bytes 524288 | tf_op jit(solution)/shard_map/psum | solution.py:39
  354.4 207.4 %all-reduce.11.cloned.1.call-start = ((), (), s32[]{:S(2)}) async-start(), calls=%async_computation.6 | async-start | bytes 524288 | tf_op jit(solution)/shard_map/psum | solution.py:39
  358.1 99.6 %copy-start.4 = (f32[64,256]{1,0:T(8,128)S(1)}, f32[64,256]{1,0:T(8,128)}, u32[]{:S(2)}) copy-start(f32[64,256]{1,0:T(8,128)} %reduce-scatter.5.cloned.1.call-done) | copy-start | bytes 196612
  358.1 101.1 %copy-start.6 = (f32[1,256]{1,0:T(1,128)S(1)}, f32[1,256]{1,0:T(1,128)}, u32[]{:S(2)}) copy-start(f32[1,256]{1,0:T(1,128)} %param.14) | copy-start | bytes 3076
  358.4 206.3 %copy-start.7 = (f32[1,256]{1,0:T(1,128)S(1)}, f32[1,256]{1,0:T(1,128)}, u32[]{:S(2)}) copy-start(f32[1,256]{1,0:T(1,128)} %param.15) | copy-start | bytes 3076
  358.4 100.8 %collective-permute-start = (f32[32,2048]{1,0:T(8,128)S(1)}, f32[32,2048]{1,0:T(8,128)S(1)}, u32[]{:S(2)}, u32[]{:S(2)}) collective-permute-start(f32[32,2048]{1,0:T(8,128)S(1)} %copy.22), channel_id=1, source_target_pairs={{0,16},{16,32},{32,48},{48,64},{64,80},{80,96},{96,112},{112,0},{1... | collective-permute-start | bytes 786440 | tf_op jit(solution)/shard_map/ppermute | solution.py:117
  358.4 101.9 %collective-permute-start.1 = (f32[32,2048]{1,0:T(8,128)S(1)}, f32[32,2048]{1,0:T(8,128)S(1)}, u32[]{:S(2)}, u32[]{:S(2)}) collective-permute-start(f32[32,2048]{1,0:T(8,128)S(1)} %copy.22), channel_id=1, source_target_pairs={{0,112},{16,0},{32,16},{48,32},{64,48},{80,64},{96,80},{112,96},{1... | collective-permute-start | bytes 786440 | tf_op jit(solution)/shard_map/ppermute | solution.py:124
  459.1 208.3 %all-reduce.13.cloned.1.call-start = ((), (), s32[]{:S(2)}) async-start(), calls=%async_computation.7 | async-start | bytes 524288 | tf_op jit(solution)/shard_map/psum | solution.py:39
  459.2 211.3 %copy-start.3 = (f32[32,2048]{1,0:T(8,128)}, f32[32,2048]{1,0:T(8,128)S(1)}, u32[]{:S(2)}) copy-start(f32[32,2048]{1,0:T(8,128)S(1)} %collective-permute-done) | copy-start | bytes 786436
  459.2 105.6 %collective-permute-start.2 = (f32[32,2048]{1,0:T(8,128)S(1)}, f32[32,2048]{1,0:T(8,128)}, u32[]{:S(2)}, u32[]{:S(2)}) collective-permute-start(f32[32,2048]{1,0:T(8,128)S(1)} %collective-permute-done), channel_id=1, source_target_pairs={{0,16},{16,32},{32,48},{48,64},{64,80},{80,96},{96,112},{112,0},{1... | collective-permute-start | bytes 786440 | tf_op jit(solution)/shard_map/ppermute | solution.py:117
  460.4 210.1 %copy-start.2 = (f32[32,2048]{1,0:T(8,128)}, f32[32,2048]{1,0:T(8,128)S(1)}, u32[]{:S(2)}) copy-start(f32[32,2048]{1,0:T(8,128)S(1)} %collective-permute-done.1) | copy-start | bytes 786436
  460.4 105.6 %collective-permute-start.3 = (f32[32,2048]{1,0:T(8,128)S(1)}, f32[32,2048]{1,0:T(8,128)}, u32[]{:S(2)}, u32[]{:S(2)}) collective-permute-start(f32[32,2048]{1,0:T(8,128)S(1)} %collective-permute-done.1), channel_id=1, source_target_pairs={{0,112},{16,0},{32,16},{48,32},{64,48},{80,64},{96,80},{112,96},{1... | collective-permute-start | bytes 786440 | tf_op jit(solution)/shard_map/ppermute | solution.py:124
  564.7 207.9 %all-reduce.15.cloned.1.call-start = ((), (), s32[]{:S(2)}) async-start(), calls=%async_computation.8 | async-start | bytes 524288 | tf_op jit(solution)/shard_map/psum | solution.py:39
  564.8 158.9 %collective-permute-start.4 = (f32[32,2048]{1,0:T(8,128)}, f32[32,2048]{1,0:T(8,128)}, u32[]{:S(2)}, u32[]{:S(2)}) collective-permute-start(f32[32,2048]{1,0:T(8,128)} %collective-permute-done.2), channel_id=1, source_target_pairs={{0,16},{16,32},{32,48},{48,64},{64,80},{80,96},{96,112},{112,0},{1... | collective-permute-start | bytes 786440 | tf_op jit(solution)/shard_map/ppermute | solution.py:117
  565.9 165.1 %collective-permute-start.5 = (f32[32,2048]{1,0:T(8,128)}, f32[32,2048]{1,0:T(8,128)}, u32[]{:S(2)}, u32[]{:S(2)}) collective-permute-start(f32[32,2048]{1,0:T(8,128)} %collective-permute-done.3), channel_id=1, source_target_pairs={{0,112},{16,0},{32,16},{48,32},{64,48},{80,64},{96,80},{112,96},{1... | collective-permute-start | bytes 786440 | tf_op jit(solution)/shard_map/ppermute | solution.py:124
  670.4 207.5 %all-reduce.17.cloned.1.call-start = ((), (), s32[]{:S(2)}) async-start(), calls=%async_computation.9 | async-start | bytes 524288 | tf_op jit(solution)/shard_map/psum | solution.py:39
  736.9 38.7 %collective-permute-start.6 = (f32[32,2048]{1,0:T(8,128)}, f32[32,2048]{1,0:T(8,128)}, u32[]{:S(2)}, u32[]{:S(2)}) collective-permute-start(f32[32,2048]{1,0:T(8,128)} %collective-permute-done.4), channel_id=1, source_target_pairs={{0,16},{16,32},{32,48},{48,64},{64,80},{80,96},{96,112},{112,0},{1... | collective-permute-start | bytes 786440 | tf_op jit(solution)/shard_map/ppermute | solution.py:117
Sparse Core Ops, SparseCore 0:
  31.7 94.4 reduce-scatter.2
  132.6 63.9 all-reduce.6
  200.9 20.3 reduce-scatter.4
  354.5 101.5 all-reduce.8
  459.8 101.9 all-reduce.10
  565.4 101.9 all-reduce.12
  670.6 101.9 all-reduce.14
  775.9 101.9 all-reduce.16
